TPU v7x, 256 devices: a whole 4x4x8 slice. The times are simulated.
256 devices in a mesh: dp: 16 (over y, x), expert: 16 (over z, core).
Axes of the slice: x: 4, y: 4, z: 8, core: 2. Of those that a mesh axis runs over, the one named last changes fastest.
Arguments:
- tokens: bfloat16 [32768, 768], P(('dp', 'expert')), may hold values from -6 to 6
- cotangent: bfloat16 [32768, 768], P(('dp', 'expert')), may hold values from -6 to 6
- routes: int32 [32768, 2], P(('dp', 'expert')), may hold values from 0 to 15, all different within a row; in each aligned block of 128 rows (0 to 127, 128 to 255, ...) at most 48 rows name the same one
- gates: float32 [32768, 2], P(('dp', 'expert')), may hold values from 0.1 to 1
- w_in: bfloat16 [16, 2304, 768], P('expert', 'dp'), may hold values from -0.21875 to 0.21875
- w_out: bfloat16 [16, 2304, 768], P('expert', 'dp'), may hold values from -0.125 to 0.125
Outputs:
- d_tokens: bfloat16 [32768, 768], P(('dp', 'expert'))
- grad_in: float32 [16, 2304, 768], P('expert', 'dp')
- grad_out: float32 [16, 2304, 768], P('expert', 'dp')
Inputs may be any that keep to these rules, and one draw needn't show every extreme that they name: `routes`: within the rows of one device (128 rows) no expert is named more than 48 times, and in every draw some expert is named exactly 48 times by the rows of some device; the 2 entries of a row differ.
All inputs are finite; a program needn't handle non-finite values.
Results may differ from a plain program's by a relative error of at most 0.015.
Values may be sent and summed in bfloat16 or wider, within the bound.
No kernel may reach another device: no remote copies, remote signals or barrier semaphores. Data moves between devices by JAX's collectives and lax.ppermute only.
A program may use at most 64 MiB of HBM per device.

v0:
```python
import jax
import jax.numpy as jnp
from jax import lax
from jax.sharding import PartitionSpec as P

tanh_coef = 0.7978845608028654
cubic_coef = 0.044715


def gelu_tanh(value):
    inner = tanh_coef * (value + cubic_coef * value * value * value)
    return 0.5 * value * (1.0 + jnp.tanh(inner))


def gelu_slope(value):
    inner = tanh_coef * (value + cubic_coef * value * value * value)
    slope_t = jnp.tanh(inner)
    return 0.5 * (1.0 + slope_t) + 0.5 * value * (1.0 - slope_t * slope_t) * tanh_coef * (
        1.0 + 3.0 * cubic_coef * value * value
    )


def dispatch_tables(route_blk, gate_blk, experts, capacity):
    tok_rows = route_blk.shape[0]
    flat = route_blk.reshape(-1)
    onehot = (flat[:, None] == jnp.arange(experts, dtype=jnp.int32)[None, :]).astype(jnp.int32)
    before = jnp.cumsum(onehot, axis=0) - onehot
    position = jnp.sum(before * onehot, axis=1)
    slots = (flat * capacity + position).reshape(tok_rows, -1)
    slot_ids = jnp.arange(experts * capacity, dtype=jnp.int32)
    placed = slot_ids[:, None, None] == slots[None, :, :]
    route_mat = jnp.sum(placed.astype(jnp.int32), axis=2).astype(jnp.bfloat16)
    gate_slot = jnp.sum(jnp.where(placed, gate_blk[None, :, :], jnp.float32(0.0)), axis=(1, 2))
    return (route_mat, gate_slot)


def shards(tokens, cotangent, routes, gates, w_in, w_out):
    experts = lax.axis_size("expert")
    tok_rows, model_width = tokens.shape
    top_count = routes.shape[1]
    capacity = 3 * tok_rows * top_count // experts
    shard_rows = w_in.shape[1]
    slot_rows = experts * capacity
    route_mat, gate_slot = dispatch_tables(routes, gates, experts, capacity)
    rows_sent = jnp.dot(route_mat, tokens, preferred_element_type=jnp.float32).astype(jnp.bfloat16)
    grad_rows = jnp.dot(route_mat, cotangent, preferred_element_type=jnp.float32)
    grads_sent = (gate_slot[:, None] * grad_rows).astype(jnp.bfloat16)
    rows_recv, grads_recv = (
        lax.all_to_all(
            rows_sent.reshape(experts, capacity, model_width),
            "expert",
            split_axis=0,
            concat_axis=0,
            tiled=True,
        ),
        lax.all_to_all(
            grads_sent.reshape(experts, capacity, model_width),
            "expert",
            split_axis=0,
            concat_axis=0,
            tiled=True,
        ),
    )
    rows_in = rows_recv.reshape(slot_rows, model_width)
    grads_in = grads_recv.reshape(slot_rows, model_width)
    piece_in = lax.all_gather(w_in[0], "dp", axis=0, tiled=True)
    piece_out = lax.all_gather(w_out[0], "dp", axis=0, tiled=True)
    pre = lax.dot_general(
        rows_in, piece_in, (((1,), (1,)), ((), ())), preferred_element_type=jnp.float32
    )
    acts = gelu_tanh(pre).astype(jnp.bfloat16)
    grad_act = lax.dot_general(
        grads_in, piece_out, (((1,), (1,)), ((), ())), preferred_element_type=jnp.float32
    )
    dpre = (grad_act * gelu_slope(pre)).astype(jnp.bfloat16)
    slot_sum = jnp.dot(dpre, piece_in, preferred_element_type=jnp.float32)
    slot_sum, acts_all, dpre_all = (slot_sum, acts, dpre)
    returned = lax.all_to_all(
        slot_sum.astype(jnp.bfloat16).reshape(experts, capacity, model_width),
        "expert",
        split_axis=0,
        concat_axis=0,
        tiled=True,
    )
    token_grads = lax.dot_general(
        route_mat,
        returned.reshape(slot_rows, model_width),
        (((0,), (0,)), ((), ())),
        preferred_element_type=jnp.float32,
    )
    d_tokens = token_grads.astype(jnp.bfloat16)
    term_in = lax.dot_general(
        dpre_all, rows_in, (((0,), (0,)), ((), ())), preferred_element_type=jnp.float32
    )
    term_out = lax.dot_general(
        acts_all, grads_in, (((0,), (0,)), ((), ())), preferred_element_type=jnp.float32
    )
    summed = lax.psum(
        jnp.concatenate([term_in, term_out], axis=1).astype(jnp.bfloat16), "dp"
    ).astype(jnp.float32)
    own_rows = lax.dynamic_slice_in_dim(summed, lax.axis_index("dp") * shard_rows, shard_rows, 0)
    grad_in = own_rows[:, :model_width][None]
    grad_out = own_rows[:, model_width:][None]
    return (d_tokens, grad_in, grad_out)


def solution(mesh):
    in_specs = (
        P(("dp", "expert"), None),
        P(("dp", "expert"), None),
        P(("dp", "expert"), None),
        P(("dp", "expert"), None),
        P("expert", "dp", None),
        P("expert", "dp", None),
    )
    out_specs = (P(("dp", "expert"), None), P("expert", "dp", None), P("expert", "dp", None))
    return jax.shard_map(shards, mesh=mesh, in_specs=in_specs, out_specs=out_specs, check_vma=False)
```

profile of v0, /device:TPU:1, one launch (start us, length us, event | category | flops | bytes accessed | tf_op | source)
XLA Modules:
  0.0 294.6 jit_solution(5425610005325512928)
XLA Ops:
  7.2 0.0 copy-start
  7.2 0.0 copy-start.2
  7.2 0.0 copy-start.1
  7.2 0.0 all-gather.7.cloned.1.call-start
  7.2 0.7 all-gather.7.cloned.1.call-update
  7.9 0.0 all-gather.5.cloned.1.call-start
  8.0 0.7 all-gather.5.cloned.1.call-update
  8.7 0.8 copy.29
  9.5 0.1 eq.39
  9.6 0.1 eq.43
  9.8 0.6 reduce-window.6
  10.4 0.2 slice_reduce_fusion
  10.6 0.1 fusion.21
  10.7 0.1 reduce_sum.30
  10.8 0.1 copy.32
  10.9 0.7 multiply_add_fusion.1
  11.6 0.1 convert_reduce_fusion
  11.7 0.0 copy-done
  11.7 1.5 convolution_convert_fusion.2
  13.2 10.0 %all-to-all-start.1 = ((bf16[16,48,768]{2,1,0:T(8,128)(2,1)}), bf16[16,48,768]{2,1,0:T(8,128)(2,1)S(1)}, u32[]{:S(2)}, u32[]{:S(2)}) async-start(bf16[16,48,768]{2,1,0:T(8,128)(2,1)} %bitcast.4), calls=%async_computation.1 | async-start | bytes 2359296 | tf_op jit(solution)/shard_map/all_to_all | solution.py:49
  23.2 0.0 copy-done.2
  23.2 0.2 select_reduce_fusion
  23.4 0.0 copy-done.1
  23.4 1.5 multiply_convert_fusion.2
  24.9 28.9 %all-to-all-done.1 = bf16[16,48,768]{2,1,0:T(8,128)(2,1)S(1)} async-done(((bf16[16,48,768]{2,1,0:T(8,128)(2,1)}), bf16[16,48,768]{2,1,0:T(8,128)(2,1)S(1)}, u32[]{:S(2)}, u32[]{:S(2)}) %all-to-all-start.1) | async-done | bytes 1179680 | tf_op jit(solution)/shard_map/all_to_all | solution.py:49
  53.8 3.7 %all-to-all-start = ((bf16[16,48,768]{2,1,0:T(8,128)(2,1)}), bf16[16,48,768]{2,1,0:T(8,128)(2,1)S(1)}, u32[]{:S(2)}, u32[]{:S(2)}) async-start(bf16[16,48,768]{2,1,0:T(8,128)(2,1)} %bitcast.1), calls=%async_computation | async-start | bytes 2359296 | tf_op jit(solution)/shard_map/all_to_all | solution.py:56
  57.5 0.2 all-reduce.2.cloned.1.call-start
  57.7 10.5 %all-gather.7.cloned.1.call-done = bf16[1,2304,768]{2,1,0:T(8,128)(2,1)} async-done(((bf16[1,144,768]{2,1,0:T(8,128)(2,1)}), bf16[1,2304,768]{2,1,0:T(8,128)(2,1)}) %all-gather.7.cloned.1.call-update) | async-done | bytes 3538960 | tf_op jit(solution)/shard_map/all_gather | solution.py:66
  68.2 7.0 %fusion.9 = f32[768,2304]{1,0:T(8,128)} fusion(bf16[768,768]{1,0:T(8,128)(2,1)S(1)} %bitcast.49, bf16[1,2304,768]{2,1,0:T(8,128)(2,1)} %all-gather.7.cloned.1.call-done), kind=kOutput, calls=%fused_computation.15 | convolution fusion | flops 2717908992 | bytes 11796480 | tf_op jit(solution)/shard_map/dot_general | solution.py:68
  75.2 12.9 %all-to-all-done = bf16[16,48,768]{2,1,0:T(8,128)(2,1)S(1)} async-done(((bf16[16,48,768]{2,1,0:T(8,128)(2,1)}), bf16[16,48,768]{2,1,0:T(8,128)(2,1)S(1)}, u32[]{:S(2)}, u32[]{:S(2)}) %all-to-all-start) | async-done | bytes 1179680 | tf_op jit(solution)/shard_map/all_to_all | solution.py:56
  88.0 8.3 %convolution_convert_fusion = bf16[2304,768]{0,1:T(8,128)(2,1)} fusion(bf16[768,768]{1,0:T(8,128)(2,1)S(1)} %bitcast.51, f32[768,2304]{1,0:T(8,128)} %fusion.9), kind=kOutput, calls=%fused_computation.11 | convolution fusion | flops 2735603712 | bytes 11796480 | tf_op jit(solution)/shard_map/dot_general | solution.py:95
  96.4 27.6 %all-gather.5.cloned.1.call-done = bf16[1,2304,768]{2,1,0:T(8,128)(2,1)} async-done(((bf16[1,144,768]{2,1,0:T(8,128)(2,1)}), bf16[1,2304,768]{2,1,0:T(8,128)(2,1)}) %all-gather.5.cloned.1.call-update) | async-done | bytes 3538960 | tf_op jit(solution)/shard_map/all_gather | solution.py:67
  124.0 8.4 %fusion.6 = bf16[768,2304]{1,0:T(8,128)(2,1)S(1)} fusion(f32[768,2304]{1,0:T(8,128)} %fusion.9, bf16[768,768]{1,0:T(8,128)(2,1)S(1)} %bitcast.52, bf16[1,2304,768]{2,1,0:T(8,128)(2,1)} %all-gather.5.cloned.1.call-done), kind=kOutput, calls=%fused_computation.8 | convolution fusion | flops 2751528960 | bytes 15335424 | tf_op jit(solution)/shard_map/dot_general | solution.py:72
  132.4 0.0 copy-start.3
  132.5 1.7 copy-done.3
  134.2 4.7 %convolution_convert_fusion.1 = bf16[2304,768]{0,1:T(8,128)(2,1)} fusion(bf16[768,2304]{1,0:T(8,128)(2,1)S(1)} %fusion.6, bf16[768,768]{1,0:T(8,128)(2,1)S(1)} %bitcast.50), kind=kOutput, calls=%fused_computation.12 | convolution fusion | flops 2719678464 | bytes 8257536 | tf_op jit(solution)/shard_map/dot_general | solution.py:92
  138.9 6.4 %pad_maximum_fusion = bf16[2304,1536]{0,1:T(8,128)(2,1)} fusion(bf16[2304,768]{0,1:T(8,128)(2,1)} %convolution_convert_fusion, bf16[2304,768]{0,1:T(8,128)(2,1)} %convolution_convert_fusion.1), kind=kLoop, calls=%fused_computation.9 | loop fusion | flops 14155776 | bytes 14155776 | tf_op jit(solution)/shard_map/concatenate | solution.py:99
  145.3 0.0 all-reduce.2.cloned.1.call-update
  145.3 7.0 %fusion.16 = bf16[768,768]{1,0:T(8,128)(2,1)} fusion(bf16[768,2304]{1,0:T(8,128)(2,1)} %copy-done.3, bf16[1,2304,768]{2,1,0:T(8,128)(2,1)} %all-gather.7.cloned.1.call-done), kind=kOutput, calls=%fused_computation.23 | convolution fusion | flops 2718498816 | bytes 8257536 | tf_op jit(solution)/shard_map/dot_general | solution.py:76
  152.3 8.1 %all-to-all-start.2 = ((bf16[16,48,768]{2,1,0:T(8,128)(2,1)}), bf16[16,48,768]{2,1,0:T(8,128)(2,1)S(1)}, u32[]{:S(2)}, u32[]{:S(2)}) async-start(bf16[16,48,768]{2,1,0:T(8,128)(2,1)} %bitcast.7), calls=%async_computation.2 | async-start | bytes 2359296 | tf_op jit(solution)/shard_map/all_to_all | solution.py:78
  160.4 30.6 %all-to-all-done.2 = bf16[16,48,768]{2,1,0:T(8,128)(2,1)S(1)} async-done(((bf16[16,48,768]{2,1,0:T(8,128)(2,1)}), bf16[16,48,768]{2,1,0:T(8,128)(2,1)S(1)}, u32[]{:S(2)}, u32[]{:S(2)}) %all-to-all-start.2) | async-done | bytes 1179680 | tf_op jit(solution)/shard_map/all_to_all | solution.py:78
  191.0 1.0 convolution_convert_fusion.3
  192.0 92.4 %all-reduce.2.cloned.1.call-done = bf16[2304,1536]{0,1:T(8,128)(2,1)} async-done(((bf16[2304,1536]{0,1:T(8,128)(2,1)}), bf16[2304,1536]{0,1:T(8,128)(2,1)}) %all-reduce.2.cloned.1.call-update) | async-done | bytes 7077904 | tf_op jit(solution)/shard_map/psum | solution.py:98
  284.4 1.6 dynamic-slice_convert_fusion
  285.9 0.1 slice_bitcast_fusion
  286.0 1.0 copy.33
  287.0 1.0 copy.34
  (3 shorter events, 0.0 us)
Async XLA Ops:
  7.2 4.5 %copy-start = (bf16[128,768]{1,0:T(8,128)(2,1)S(1)}, bf16[128,768]{1,0:T(8,128)(2,1)}, u32[]{:S(2)}) copy-start(bf16[128,768]{1,0:T(8,128)(2,1)} %param.6) | copy-start | bytes 589828
  7.2 16.0 %copy-start.2 = (f32[128,2]{0,1:T(2,128)S(1)}, f32[128,2]{0,1:T(2,128)}, u32[]{:S(2)}) copy-start(f32[128,2]{0,1:T(2,128)} %param.9) | copy-start | bytes 3076
  7.2 16.2 %copy-start.1 = (bf16[128,768]{1,0:T(8,128)(2,1)S(1)}, bf16[128,768]{1,0:T(8,128)(2,1)}, u32[]{:S(2)}) copy-start(bf16[128,768]{1,0:T(8,128)(2,1)} %param.7) | copy-start | bytes 589828
  7.2 61.0 %all-gather.7.cloned.1.call-start = ((), (), s32[]{:S(2)}) async-start(), calls=%async_computation.5 | async-start | bytes 3760128 | tf_op jit(solution)/shard_map/all_gather | solution.py:66
  7.9 116.1 %all-gather.5.cloned.1.call-start = ((), (), s32[]{:S(2)}) async-start(), calls=%async_computation.4 | async-start | bytes 3760128 | tf_op jit(solution)/shard_map/all_gather | solution.py:67
  13.2 40.5 %all-to-all-start.1 = ((bf16[16,48,768]{2,1,0:T(8,128)(2,1)}), bf16[16,48,768]{2,1,0:T(8,128)(2,1)S(1)}, u32[]{:S(2)}, u32[]{:S(2)}) async-start(bf16[16,48,768]{2,1,0:T(8,128)(2,1)} %bitcast.4), calls=%async_computation.1 | async-start | bytes 2359296 | tf_op jit(solution)/shard_map/all_to_all | solution.py:49
  53.8 34.3 %all-to-all-start = ((bf16[16,48,768]{2,1,0:T(8,128)(2,1)}), bf16[16,48,768]{2,1,0:T(8,128)(2,1)S(1)}, u32[]{:S(2)}, u32[]{:S(2)}) async-start(bf16[16,48,768]{2,1,0:T(8,128)(2,1)} %bitcast.1), calls=%async_computation | async-start | bytes 2359296 | tf_op jit(solution)/shard_map/all_to_all | solution.py:56
  57.5 226.9 %all-reduce.2.cloned.1.call-start = ((), (), s32[]{:S(2)}) async-start(), calls=%async_computation.3 | async-start | bytes 14155776 | tf_op jit(solution)/shard_map/psum | solution.py:98
  132.4 1.8 copy-start.3
  152.3 38.6 %all-to-all-start.2 = ((bf16[16,48,768]{2,1,0:T(8,128)(2,1)}), bf16[16,48,768]{2,1,0:T(8,128)(2,1)S(1)}, u32[]{:S(2)}, u32[]{:S(2)}) async-start(bf16[16,48,768]{2,1,0:T(8,128)(2,1)} %bitcast.7), calls=%async_computation.2 | async-start | bytes 2359296 | tf_op jit(solution)/shard_map/all_to_all | solution.py:78
Sparse Core Ops, SparseCore 0:
  10.5 57.6 all-gather.6
  70.6 53.3 all-gather.4
  145.5 138.8 all-reduce.1
where the time goes:
time: 295 us
  waiting for transfers between devices  204 us (69%)
  matrix products  39.5 us (13%)
  starting transfers between devices  22 us (7%)
  between operations  13.8 us (5%)
  other arithmetic  9.72 us (3%)
  local copies, waits for them, and re-layouts  5.32 us (2%)
    psum x1, waiting for transfers between devices, shards(): lax.psum(jnp.concatenate([term_in, term_out], axis=1).astype(jnp.bfloat16...  92.4 us
    all_to_all x1, waiting for transfers between devices, shards(): lax.all_to_all(slot_sum.astype(jnp.bfloat16).reshape(experts, capacity, m...  30.6 us
    all_to_all x1, waiting for transfers between devices, shards(): lax.all_to_all(rows_sent.reshape(experts, capacity, model_width), 'expert...  28.9 us
    all_gather x1, waiting for transfers between devices, shards(): piece_out = lax.all_gather(w_out[0], 'dp', axis=0, tiled=True)  27.6 us
    all_to_all x1, waiting for transfers between devices, shards(): lax.all_to_all(grads_sent.reshape(experts, capacity, model_width), 'exper...  12.9 us
    all_gather x1, waiting for transfers between devices, shards(): piece_in = lax.all_gather(w_in[0], 'dp', axis=0, tiled=True)  10.5 us
    all_to_all x1, starting transfers between devices, shards(): lax.all_to_all(rows_sent.reshape(experts, capacity, model_width), 'expert...  9.98 us
    dot_general x1, matrix products, shards(): lax.dot_general(grads_in, piece_out, (((1,), (1,)), ((), ())), preferred_...  8.45 us
  transfers between devices with their start and end apart: 6, of which 6 were waited for; matrix products, arithmetic and copies ran while one was open for 10% of the time, Pallas kernels for 0%

commit v1 on v0

--- a/solution.py
+++ b/solution.py
@@ -64,7 +64,9 @@
     rows_in = rows_recv.reshape(slot_rows, model_width)
     grads_in = grads_recv.reshape(slot_rows, model_width)
     piece_in = lax.all_gather(w_in[0], "dp", axis=0, tiled=True)
-    piece_out = lax.all_gather(w_out[0], "dp", axis=0, tiled=True)
+    block = w_out[0]
+    sent = jnp.stack([block] * lax.axis_size("dp"))
+    piece_out = jnp.concatenate(lax.all_to_all(sent, "dp", 0, 0), axis=0)
     pre = lax.dot_general(
         rows_in, piece_in, (((1,), (1,)), ((), ())), preferred_element_type=jnp.float32
     )

time: 295 us -> 318 us (1.078)
  blocking collectives: 0 us -> 35.1 us
  waiting for transfers between devices: 204 us -> 193 us
  matrix products: 39.5 us -> 33.4 us
  local copies, waits for them, and re-layouts: 5.32 us -> 10.2 us
    all_to_all x0 -> x1, blocking collectives: none -> 35.1 us  [shards(): lax.all_to_all(rows_sent.reshape(experts, capacity, model_width), 'expert...]
    all_gather x1 -> x0, waiting for transfers between devices: 27.6 us -> none  [shards(): piece_out = lax.all_gather(w_out[0], 'dp', axis=0, tiled=True)]
    all_to_all x1, waiting for transfers between devices: 12.9 us -> 30.1 us  [shards(): lax.all_to_all(grads_sent.reshape(experts, capacity, model_width), 'exper...]
    all_to_all x1, waiting for transfers between devices: 28.9 us -> 41.2 us  [shards(): piece_out = jnp.concatenate(lax.all_to_all(sent, 'dp', 0, 0), axis=0)]
    all_gather x1, waiting for transfers between devices: 10.5 us -> 0.02 us  [shards(): piece_in = lax.all_gather(w_in[0], 'dp', axis=0, tiled=True)]
    all_to_all x1, starting transfers between devices: 3.7 us -> 10.1 us  [shards(): lax.all_to_all(grads_sent.reshape(experts, capacity, model_width), 'exper...]
    all_to_all x1, starting transfers between devices: 8.06 us -> 4.35 us  [shards(): lax.all_to_all(slot_sum.astype(jnp.bfloat16).reshape(experts, capacity, m...]
    unnamed x11 -> x19, local copies, waits for them, and re-layouts: 4.55 us -> 7.48 us
  transfers between devices with their start and end apart: 6 -> 5, of which waited for: 6 -> 4; matrix products, arithmetic and copies ran while one was open for 10% -> 8% of each run, Pallas kernels for 0% -> 0%
where the time goes in v1:
time: 318 us; the launch traced here: 317 us
  waiting for transfers between devices  193 us (61%)
  blocking collectives  35.1 us (11%)
  matrix products  33.4 us (11%)
  starting transfers between devices  21.6 us (7%)
  between operations  14.2 us (4%)
  local copies, waits for them, and re-layouts  10.2 us (3%)
  other arithmetic  9.31 us (3%)
    psum x1, waiting for transfers between devices, shards(): lax.psum(jnp.concatenate([term_in, term_out], axis=1).astype(jnp.bfloat16...  90.7 us
    all_to_all x1, waiting for transfers between devices, shards(): piece_out = jnp.concatenate(lax.all_to_all(sent, 'dp', 0, 0), axis=0)  41.2 us
    all_to_all x1, blocking collectives, shards(): lax.all_to_all(rows_sent.reshape(experts, capacity, model_width), 'expert...  35.1 us
    all_to_all x1, waiting for transfers between devices, shards(): lax.all_to_all(slot_sum.astype(jnp.bfloat16).reshape(experts, capacity, m...  30.6 us
    all_to_all x1, waiting for transfers between devices, shards(): lax.all_to_all(grads_sent.reshape(experts, capacity, model_width), 'exper...  30.1 us
    all_to_all x1, starting transfers between devices, shards(): lax.all_to_all(grads_sent.reshape(experts, capacity, model_width), 'exper...  10.1 us
    dot_general x1, matrix products, shards(): lax.dot_general(grads_in, piece_out, (((1,), (1,)), ((), ())), preferred_...  8.45 us
    unnamed x19, local copies, waits for them, and re-layouts  7.48 us
  transfers between devices with their start and end apart: 5, of which 4 were waited for; matrix products, arithmetic and copies ran while one was open for 8% of the time, Pallas kernels for 0%

profile of v1, /device:TPU:1, one launch (start us, length us, event | category | flops | bytes accessed | tf_op | source)
XLA Modules:
  0.0 317.2 jit_solution(10296061607794248278)
XLA Ops:
  7.2 0.0 copy-start
  7.2 0.0 copy-start.5
  7.2 0.0 all-gather.3.cloned.1.call-start
  7.2 0.7 all-gather.3.cloned.1.call-update
  7.9 0.8 copy.29
  8.7 0.1 eq.43
  8.9 0.1 eq.39
  9.0 0.6 reduce-window.6
  9.6 0.2 slice_reduce_fusion
  9.8 0.1 fusion.20
  9.9 0.1 reduce_sum.30
  10.1 0.1 copy.32
  10.1 0.7 multiply_add_fusion.1
  10.8 0.1 convert_reduce_fusion
  10.9 0.9 select_reduce_fusion
  11.8 0.0 copy-done
  11.8 1.5 multiply_convert_fusion.2
  13.3 0.0 copy-start.4
  13.3 10.1 %all-to-all-start = ((bf16[16,48,768]{2,1,0:T(8,128)(2,1)}), bf16[16,48,768]{2,1,0:T(8,128)(2,1)S(1)}, u32[]{:S(2)}, u32[]{:S(2)}) async-start(bf16[16,48,768]{2,1,0:T(8,128)(2,1)} %bitcast.1), calls=%async_computation | async-start | bytes 2359296 | tf_op jit(solution)/shard_map/all_to_all | solution.py:56
  23.4 0.0 copy-done.5
  23.4 0.4 convolution_convert_fusion.2
  23.9 30.1 %all-to-all-done = bf16[16,48,768]{2,1,0:T(8,128)(2,1)S(1)} async-done(((bf16[16,48,768]{2,1,0:T(8,128)(2,1)}), bf16[16,48,768]{2,1,0:T(8,128)(2,1)S(1)}, u32[]{:S(2)}, u32[]{:S(2)}) %all-to-all-start) | async-done | bytes 1179680 | tf_op jit(solution)/shard_map/all_to_all | solution.py:56
  54.0 35.1 %all_to_all.20 = bf16[16,48,768]{2,1,0:T(8,128)(2,1)} all-to-all(bf16[16,48,768]{2,1,0:T(8,128)(2,1)S(1)} %bitcast.49), channel_id=1, replica_groups=mesh['dp'=16,'expert'=16] {'expert'}, dimensions={0} | all-to-all | bytes 2359296 | tf_op jit(solution)/shard_map/all_to_all | solution.py:49
  89.0 0.0 copy-done.4
  89.0 2.0 stack.3
  91.0 0.0 copy-start.2
  91.0 6.9 %all-to-all-start.1 = ((bf16[16,144,768]{2,1,0:T(8,128)(2,1)}), bf16[16,144,768]{2,1,0:T(8,128)(2,1)}, u32[]{:S(2)}, u32[]{:S(2)}) async-start(bf16[16,144,768]{2,1,0:T(8,128)(2,1)} %stack.3), calls=%async_computation.1 | async-start | bytes 7077888 | tf_op jit(solution)/shard_map/all_to_all | solution.py:69
  98.0 0.2 all-reduce.2.cloned.1.call-start
  98.2 0.0 all-gather.3.cloned.1.call-done
  98.2 0.0 copy-done.2
  98.2 4.9 %fusion.9 = f32[768,2304]{1,0:T(8,128)S(1)} fusion(bf16[768,768]{1,0:T(8,128)(2,1)S(1)} %bitcast.52, bf16[1,2304,768]{2,1,0:T(8,128)(2,1)} %all-gather.3.cloned.1.call-done), kind=kOutput, calls=%fused_computation.15 | convolution fusion | flops 2717908992 | bytes 11796480 | tf_op jit(solution)/shard_map/dot_general | solution.py:70
  103.2 0.0 copy-start.6
  103.2 2.9 copy-done.6
  106.1 5.4 %convolution_convert_fusion = bf16[2304,768]{0,1:T(8,128)(2,1)} fusion(bf16[768,768]{1,0:T(8,128)(2,1)S(1)} %bitcast.50, f32[768,2304]{1,0:T(8,128)S(1)} %fusion.9), kind=kOutput, calls=%fused_computation.11 | convolution fusion | flops 2735603712 | bytes 11796480 | tf_op jit(solution)/shard_map/dot_general | solution.py:97
  111.5 41.2 %all-to-all-done.1 = bf16[16,144,768]{2,1,0:T(8,128)(2,1)} async-done(((bf16[16,144,768]{2,1,0:T(8,128)(2,1)}), bf16[16,144,768]{2,1,0:T(8,128)(2,1)}, u32[]{:S(2)}, u32[]{:S(2)}) %all-to-all-start.1) | async-done | bytes 3538976 | tf_op jit(solution)/shard_map/all_to_all | solution.py:69
  152.6 0.0 copy-start.3
  152.6 8.5 %fusion.6 = bf16[768,2304]{1,0:T(8,128)(2,1)S(1)} fusion(f32[768,2304]{1,0:T(8,128)} %copy-done.6, bf16[768,768]{1,0:T(8,128)(2,1)S(1)} %bitcast.51, bf16[2304,768]{1,0:T(8,128)(2,1)} %bitcast.4), kind=kOutput, calls=%fused_computation.8 | convolution fusion | flops 2751528960 | bytes 15335424 | tf_op jit(solution)/shard_map/dot_general | solution.py:74
  161.1 0.0 copy-start.7
  161.1 1.8 copy-done.7
  162.8 0.0 copy-done.3
  162.8 0.0 copy-start.1
  162.9 4.7 %convolution_convert_fusion.1 = bf16[2304,768]{0,1:T(8,128)(2,1)} fusion(bf16[768,2304]{1,0:T(8,128)(2,1)S(1)} %fusion.6, bf16[768,768]{1,0:T(8,128)(2,1)S(1)} %bitcast.53), kind=kOutput, calls=%fused_computation.12 | convolution fusion | flops 2719678464 | bytes 8257536 | tf_op jit(solution)/shard_map/dot_general | solution.py:94
  167.5 0.0 copy-done.1
  167.5 5.4 %pad_maximum_fusion = bf16[2304,1536]{0,1:T(8,128)(2,1)} fusion(bf16[2304,768]{0,1:T(8,128)(2,1)S(1)} %copy-done.1, bf16[2304,768]{0,1:T(8,128)(2,1)} %convolution_convert_fusion.1), kind=kLoop, calls=%fused_computation.9 | loop fusion | flops 14155776 | bytes 14155776 | tf_op jit(solution)/shard_map/concatenate | solution.py:101
  172.9 0.0 all-reduce.2.cloned.1.call-update
  172.9 7.0 %fusion.15 = bf16[768,768]{1,0:T(8,128)(2,1)} fusion(bf16[768,2304]{1,0:T(8,128)(2,1)} %copy-done.7, bf16[1,2304,768]{2,1,0:T(8,128)(2,1)} %all-gather.3.cloned.1.call-done), kind=kOutput, calls=%fused_computation.22 | convolution fusion | flops 2718498816 | bytes 8257536 | tf_op jit(solution)/shard_map/dot_general | solution.py:78
  180.0 4.3 %all-to-all-start.3 = ((bf16[16,48,768]{2,1,0:T(8,128)(2,1)}), bf16[16,48,768]{2,1,0:T(8,128)(2,1)S(1)}, u32[]{:S(2)}, u32[]{:S(2)}) async-start(bf16[16,48,768]{2,1,0:T(8,128)(2,1)} %bitcast.8), calls=%async_computation.3 | async-start | bytes 2359296 | tf_op jit(solution)/shard_map/all_to_all | solution.py:80
  184.3 30.6 %all-to-all-done.3 = bf16[16,48,768]{2,1,0:T(8,128)(2,1)S(1)} async-done(((bf16[16,48,768]{2,1,0:T(8,128)(2,1)}), bf16[16,48,768]{2,1,0:T(8,128)(2,1)S(1)}, u32[]{:S(2)}, u32[]{:S(2)}) %all-to-all-start.3) | async-done | bytes 1179680 | tf_op jit(solution)/shard_map/all_to_all | solution.py:80
  214.9 1.0 convolution_convert_fusion.3
  215.9 90.7 %all-reduce.2.cloned.1.call-done = bf16[2304,1536]{0,1:T(8,128)(2,1)} async-done(((bf16[2304,1536]{0,1:T(8,128)(2,1)}), bf16[2304,1536]{0,1:T(8,128)(2,1)}) %all-reduce.2.cloned.1.call-update) | async-done | bytes 7077904 | tf_op jit(solution)/shard_map/psum | solution.py:100
  306.7 1.6 dynamic-slice_convert_fusion
  308.2 0.1 slice_bitcast_fusion
  308.3 1.0 copy.34
  309.3 1.0 copy.33
  (3 shorter events, 0.0 us)
Async XLA Ops:
  7.2 4.6 %copy-start = (bf16[128,768]{1,0:T(8,128)(2,1)S(1)}, bf16[128,768]{1,0:T(8,128)(2,1)}, u32[]{:S(2)}) copy-start(bf16[128,768]{1,0:T(8,128)(2,1)} %param.7) | copy-start | bytes 589828
  7.2 16.2 %copy-start.5 = (bf16[128,768]{1,0:T(8,128)(2,1)S(1)}, bf16[128,768]{1,0:T(8,128)(2,1)}, u32[]{:S(2)}) copy-start(bf16[128,768]{1,0:T(8,128)(2,1)} %param.6) | copy-start | bytes 589828
  7.2 91.0 %all-gather.3.cloned.1.call-start = ((), (), s32[]{:S(2)}) async-start(), calls=%async_computation.5 | async-start | bytes 3760128 | tf_op jit(solution)/shard_map/all_gather | solution.py:66
  13.3 75.7 %copy-start.4 = (bf16[1,144,768]{2,1,0:T(8,128)(2,1)S(1)}, bf16[1,144,768]{2,1,0:T(8,128)(2,1)}, u32[]{:S(2)}) copy-start(bf16[1,144,768]{2,1,0:T(8,128)(2,1)} %param.11) | copy-start | bytes 663556
  13.3 40.7 %all-to-all-start = ((bf16[16,48,768]{2,1,0:T(8,128)(2,1)}), bf16[16,48,768]{2,1,0:T(8,128)(2,1)S(1)}, u32[]{:S(2)}, u32[]{:S(2)}) async-start(bf16[16,48,768]{2,1,0:T(8,128)(2,1)} %bitcast.1), calls=%async_computation | async-start | bytes 2359296 | tf_op jit(solution)/shard_map/all_to_all | solution.py:56
  91.0 7.2 %copy-start.2 = (bf16[16,48,768]{2,1,0:T(8,128)(2,1)S(1)}, bf16[16,48,768]{2,1,0:T(8,128)(2,1)}, u32[]{:S(2)}) copy-start(bf16[16,48,768]{2,1,0:T(8,128)(2,1)} %all_to_all.20) | copy-start | bytes 3538948
  91.0 61.6 %all-to-all-start.1 = ((bf16[16,144,768]{2,1,0:T(8,128)(2,1)}), bf16[16,144,768]{2,1,0:T(8,128)(2,1)}, u32[]{:S(2)}, u32[]{:S(2)}) async-start(bf16[16,144,768]{2,1,0:T(8,128)(2,1)} %stack.3), calls=%async_computation.1 | async-start | bytes 7077888 | tf_op jit(solution)/shard_map/all_to_all | solution.py:69
  98.0 208.7 %all-reduce.2.cloned.1.call-start = ((), (), s32[]{:S(2)}) async-start(), calls=%async_computation.4 | async-start | bytes 14155776 | tf_op jit(solution)/shard_map/psum | solution.py:100
  103.2 2.9 copy-start.6
  152.6 10.2 %copy-start.3 = (bf16[16,48,768]{2,1,0:T(8,128)(2,1)S(1)}, bf16[16,48,768]{2,1,0:T(8,128)(2,1)}, u32[]{:S(2)}) copy-start(bf16[16,48,768]{2,1,0:T(8,128)(2,1)} %all_to_all.20) | copy-start | bytes 3538948
  161.1 1.8 copy-start.7
  162.8 4.7 %copy-start.1 = (bf16[2304,768]{0,1:T(8,128)(2,1)S(1)}, bf16[2304,768]{0,1:T(8,128)(2,1)}, u32[]{:S(2)}) copy-start(bf16[2304,768]{0,1:T(8,128)(2,1)} %convolution_convert_fusion) | copy-start | bytes 10616836
  180.0 35.0 %all-to-all-start.3 = ((bf16[16,48,768]{2,1,0:T(8,128)(2,1)}), bf16[16,48,768]{2,1,0:T(8,128)(2,1)S(1)}, u32[]{:S(2)}, u32[]{:S(2)}) async-start(bf16[16,48,768]{2,1,0:T(8,128)(2,1)} %bitcast.8), calls=%async_computation.3 | async-start | bytes 2359296 | tf_op jit(solution)/shard_map/all_to_all | solution.py:80
Sparse Core Ops, SparseCore 0:
  10.5 57.6 all-gather.2
  173.1 133.5 all-reduce.1
